TPU v7x, 256 devices: a whole 4x4x8 slice. The times are simulated.
256 devices in a mesh: row: 32 (over z, y), col: 8 (over x, core).
Axes of the slice: x: 4, y: 4, z: 8, core: 2. Of those that a mesh axis runs over, the one named last changes fastest.
Arguments:
- amps: bfloat16 [30720, 30720], P(('col', 'row')), may hold values from -6 to 6
- cycle_int: bfloat16 [30720, 1024], P('col'), may hold values from -0.03125 to 0.03125
- tile_mask: int32 [480, 16], P('col'), may hold values 0 or 1
- coulomb: bfloat16 [30720, 1024], P('row', 'col'), may hold values from -6 to 6
- occ_irrep: int32 [240], replicated, may hold values from 0 to 7
- vir_irrep: int32 [192], replicated, may hold values from 0 to 7
- occ_energy: float32 [240], replicated, may hold values from -1.5 to -0.3
- vir_energy: float32 [192], replicated, may hold values from 0.3 to 2
Outputs:
- new_amps: bfloat16 [30720, 1024], P('row', 'col')
All inputs are finite; a program needn't handle non-finite values. No bound on the sum of `tile_mask` on one device may be relied on, other than what follows from the above.
Results may differ from a plain program's by a relative error of at most 0.001.
Values may be sent and summed in bfloat16 or wider, within the bound.
No kernel may reach another device: no remote copies, remote signals or barrier semaphores. Data moves between devices by JAX's collectives and lax.ppermute only.
A program may use at most 128 MiB of HBM per device.

v0:
```python
import jax
import jax.numpy as jnp
from jax import lax
from jax.sharding import Mesh, PartitionSpec as P

BLK = 64
CHUNKS = 2
Z, Y, X, C = ("z", "y", "x", "core")
COL = (X, C)
ROW = (Z, Y)


def lookup(positions, values_table):
    entries = jnp.arange(values_table.shape[0], dtype=jnp.int32)
    picked = jnp.where(
        positions[:, None] == entries[None, :],
        values_table[None, :],
        jnp.zeros((), values_table.dtype),
    )
    return jnp.sum(picked, axis=1)


def swap_perm(nz, nc):
    return [(z * nc + c, c * nz + z) for z in range(nz) for c in range(nc)]


def local(amps, cycle_int, tile_mask, coulomb, occ_irrep, vir_irrep, occ_energy, vir_energy):
    block_size = BLK
    occupied = occ_energy.shape[0]
    row_blocks = vir_energy.shape[0] // block_size - 1
    kc_rows, jb_all = cycle_int.shape
    rows_here, cols_here = coulomb.shape
    nz = lax.axis_size(Z)
    ny = lax.axis_size(Y)
    ncol = lax.axis_size(COL)
    z = lax.axis_index(Z)
    y = lax.axis_index(Y)
    c = lax.axis_index(COL)
    sub = amps.shape[0]
    span = sub * ny
    ci_rows = lax.dynamic_slice_in_dim(cycle_int, z * span, span, axis=0)
    mask_rows = jnp.repeat(tile_mask.astype(jnp.bfloat16), block_size, axis=0)
    mask_rows = lax.dynamic_slice_in_dim(mask_rows, z * span, span, axis=0)
    masked = (
        ci_rows.reshape(span, jb_all // block_size, block_size) * mask_rows[:, :, None]
    ).reshape(span, jb_all)
    masked_all = lax.all_gather(masked, COL, axis=0, tiled=True)
    groups = lax.axis_size((X, C, Y))
    width = amps.shape[1] // groups // CHUNKS
    pieces = amps.reshape(sub, groups, CHUNKS, width)
    sums = []
    previous = None
    for k in range(CHUNKS):
        piece = pieces[:, :, k, :].reshape(sub, groups * width)
        if previous is not None:
            previous, piece = lax.optimization_barrier((previous, piece))
            sums.append(lax.psum_scatter(previous, Z, scatter_dimension=1, tiled=True))
        plane_amps = lax.all_to_all(piece, (X, C, Y), split_axis=1, concat_axis=0, tiled=True)
        previous = lax.dot_general(
            plane_amps, masked_all, (((0,), (0,)), ((), ())), preferred_element_type=jnp.float32
        )
    sums.append(lax.psum_scatter(previous, Z, scatter_dimension=1, tiled=True))
    cycle_sum = jnp.concatenate(sums, axis=0)
    perm = swap_perm(nz, ncol)
    coulomb_here = lax.ppermute(coulomb, (Z, X, C), perm)
    row_block = c * ny + y
    row_pos = row_block * rows_here + jnp.arange(rows_here, dtype=jnp.int32)
    col_pos = z * cols_here + jnp.arange(cols_here, dtype=jnp.int32)
    occ_row = row_pos // block_size % occupied
    vir_row = block_size * (row_pos // (occupied * block_size)) + row_pos % block_size
    occ_col = col_pos // block_size % occupied
    vir_col = col_pos % block_size + row_blocks * block_size
    sym_row = jnp.bitwise_xor(lookup(occ_row, occ_irrep), lookup(vir_row, vir_irrep))
    sym_col = jnp.bitwise_xor(lookup(occ_col, occ_irrep), lookup(vir_col, vir_irrep))
    allowed = sym_row[:, None] == sym_col[None, :]
    gap_row = lookup(vir_row, vir_energy) - lookup(occ_row, occ_energy)
    gap_col = lookup(vir_col, vir_energy) - lookup(occ_col, occ_energy)
    denominator = gap_row[:, None] + gap_col[None, :]
    updated = (coulomb_here.astype(jnp.float32) + cycle_sum) / denominator
    out = jnp.where(allowed, updated, jnp.float32(0.0)).astype(jnp.bfloat16)
    return lax.ppermute(out, (Z, X, C), perm)


def solution(mesh):
    nrow, ncol = mesh.devices.shape
    ncore = 2
    nx = ncol // ncore
    nz = ncol
    ny = nrow // nz
    torus = Mesh(mesh.devices.reshape(nz, ny, nx, ncore), (Z, Y, X, C))
    return jax.shard_map(
        local,
        mesh=torus,
        in_specs=(P(COL + ROW, None), P(COL, None), P(COL, None), P(ROW, COL), P(), P(), P(), P()),
        out_specs=P(ROW, COL),
        check_vma=False,
    )
```

profile of v0, /device:TPU:31, one launch (start us, length us, event | category | flops | bytes accessed | tf_op | source)
XLA Modules:
  0.0 278.5 jit_solution(2675612284590024433)
XLA Ops:
  6.5 1.3 constant_dynamic-slice_fusion
  7.8 0.5 copy.42
  8.4 0.2 broadcast_in_dim.140
  8.6 0.3 reshape.126
  9.0 1.3 copy.29
  10.4 10.1 %copy.30 = bf16[120,30720]{0,1:T(8,128)(2,1)} copy(bf16[120,30720]{1,0:T(8,128)(2,1)} %param.8) | data formatting | bytes 14745600 | tf_op args[0]
  20.5 5.7 %fusion.12 = (bf16[120,32,1,480]{0,3,2,1:T(8,128)(2,1)}, bf16[120,32,480]{0,2,1:T(8,128)(2,1)}) fusion(bf16[120,32,2,480]{0,3,2,1:T(8,128)(2,1)} %bitcast.21), kind=kLoop, calls=%fused_computation.47 | loop fusion | bytes 14745600 | tf_op jit(solution)/shard_map/slice | solution.py:54
  26.1 6.5 %copy.32 = bf16[120,32,480]{2,0,1:T(8,128)(2,1)} copy(bf16[120,32,480]{0,2,1:T(8,128)(2,1)} %get-tuple-element.10) | data formatting | bytes 7372800 | tf_op jit(solution)/shard_map/all_to_all | solution.py:58
  32.6 7.7 %all-to-all-start = ((bf16[120,32,480]{2,0,1:T(8,128)(2,1)}), bf16[120,32,480]{2,0,1:T(8,128)(2,1)}, u32[]{:S(2)}, u32[]{:S(2)}) async-start(bf16[120,32,480]{2,0,1:T(8,128)(2,1)} %copy.32), calls=%async_computation | async-start | bytes 7864320 | tf_op jit(solution)/shard_map/all_to_all | solution.py:58
  40.3 6.2 %copy.40 = bf16[120,15360]{1,0:T(8,128)(2,1)} copy(bf16[120,15360]{0,1:T(8,128)(2,1)} %bitcast.23) | data formatting | bytes 7372800 | tf_op jit(solution)/shard_map/reshape;squeeze | solution.py:54
  46.5 58.6 %all-to-all-done = bf16[120,32,480]{2,0,1:T(8,128)(2,1)} async-done(((bf16[120,32,480]{2,0,1:T(8,128)(2,1)}), bf16[120,32,480]{2,0,1:T(8,128)(2,1)}, u32[]{:S(2)}, u32[]{:S(2)}) %all-to-all-start) | async-done | bytes 3686432 | tf_op jit(solution)/shard_map/all_to_all | solution.py:58
  105.1 9.7 %convolution_bitcast_fusion = f32[480,1024]{1,0:T(8,128)} fusion(bf16[3840,480]{1,0:T(8,128)(2,1)} %bitcast.4, bf16[3840,1024]{1,0:T(8,128)(2,1)} %all-gather.2.cloned.1.call-done), kind=kOutput, calls=%fused_computation.1 | convolution fusion | flops 3774873600 | bytes 13516800 | tf_op jit(solution)/shard_map/dot_general | solution.py:59
  114.8 6.1 %copy.41 = bf16[120,15360]{0,1:T(8,128)(2,1)} copy(bf16[120,15360]{1,0:T(8,128)(2,1)} %copy.40) | data formatting | bytes 7372800 | tf_op jit(solution)/shard_map/all_to_all | solution.py:58
  120.9 7.1 %all-to-all-start.1 = ((bf16[120,32,480]{0,2,1:T(8,128)(2,1)}), bf16[120,32,480]{0,2,1:T(8,128)(2,1)}, u32[]{:S(2)}, u32[]{:S(2)}) async-start(bf16[120,32,480]{0,2,1:T(8,128)(2,1)} %bitcast.22), calls=%async_computation.2 | async-start | bytes 7864320 | tf_op jit(solution)/shard_map/all_to_all | solution.py:58
  128.0 0.7 reduce-scatter.3.cloned.1.call-update
  128.8 46.8 %all-to-all-done.1 = bf16[120,32,480]{0,2,1:T(8,128)(2,1)} async-done(((bf16[120,32,480]{0,2,1:T(8,128)(2,1)}), bf16[120,32,480]{0,2,1:T(8,128)(2,1)}, u32[]{:S(2)}, u32[]{:S(2)}) %all-to-all-start.1) | async-done | bytes 3686432 | tf_op jit(solution)/shard_map/all_to_all | solution.py:58
  175.6 5.6 %copy.36 = bf16[32,120,480]{1,0,2:T(8,128)(2,1)} copy(bf16[32,120,480]{1,2,0:T(8,128)(2,1)} %bitcast.8) | data formatting | bytes 7372800 | tf_op jit(solution)/shard_map/all_to_all | solution.py:58
  181.2 8.6 %all_to_all.35 = bf16[3840,480]{0,1:T(8,128)(2,1)} reshape(bf16[32,120,480]{1,0,2:T(8,128)(2,1)} %copy.36) | data formatting | bytes 7372800 | tf_op jit(solution)/shard_map/all_to_all | solution.py:58
  189.9 9.7 %fusion.13 = f32[480,1024]{1,0:T(8,128)} fusion(bf16[3840,480]{0,1:T(8,128)(2,1)} %all_to_all.35, bf16[3840,1024]{1,0:T(8,128)(2,1)} %all-gather.2.cloned.1.call-done), kind=kOutput, calls=%fused_computation.48 | convolution fusion | flops 3774873600 | bytes 13516800 | tf_op jit(solution)/shard_map/dot_general | solution.py:59
  199.6 6.6 %collective-permute-start = (bf16[960,128]{1,0:T(8,128)(2,1)S(1)}, bf16[960,128]{1,0:T(8,128)(2,1)S(1)}, u32[]{:S(2)}, u32[]{:S(2)}) collective-permute-start(bf16[960,128]{1,0:T(8,128)(2,1)S(1)} %copy-done.5), channel_id=1, source_target_pairs={{0,0},{1,32},{2,64},{3,96},{4,128},{5,160},{6,192},{7,224},{32,1},... | collective-permute-start | bytes 737288 | tf_op jit(solution)/shard_map/ppermute | solution.py:65
  206.4 0.1 select_reduce_fusion.4
  206.5 0.2 select_reduce_fusion.2
  206.7 0.4 select_reduce_fusion
  207.2 0.1 select_reduce_fusion.5
  207.3 0.2 select_reduce_fusion.3
  207.5 0.4 select_reduce_fusion.1
  207.9 18.8 %collective-permute-done = bf16[960,128]{1,0:T(8,128)(2,1)S(1)} collective-permute-done((bf16[960,128]{1,0:T(8,128)(2,1)S(1)}, bf16[960,128]{1,0:T(8,128)(2,1)S(1)}, u32[]{:S(2)}, u32[]{:S(2)}) %collective-permute-start) | collective-permute-done | bytes 245792 | tf_op jit(solution)/shard_map/ppermute | solution.py:65
  226.7 19.3 %reduce-scatter.5.cloned.1.call-done = f32[480,128]{1,0:T(8,128)} async-done(((f32[480,1024]{1,0:T(8,128)}), f32[480,128]{1,0:T(8,128)}) %reduce-scatter.5.cloned.1.call-update) | async-done | bytes 245776 | tf_op jit(solution)/shard_map/reduce_scatter | solution.py:62
  246.0 1.4 fusion.2
  247.4 7.2 %collective-permute-start.1 = (bf16[960,128]{1,0:T(8,128)(2,1)S(1)}, bf16[960,128]{1,0:T(8,128)(2,1)S(1)}, u32[]{:S(2)}, u32[]{:S(2)}) collective-permute-start(bf16[960,128]{1,0:T(8,128)(2,1)S(1)} %fusion.2), channel_id=1, source_target_pairs={{0,0},{1,32},{2,64},{3,96},{4,128},{5,160},{6,192},{7,224},{32,1},... | collective-permute-start | bytes 737288 | tf_op jit(solution)/shard_map/ppermute | solution.py:81
  254.6 16.7 %collective-permute-done.1 = bf16[960,128]{1,0:T(8,128)(2,1)S(1)} collective-permute-done((bf16[960,128]{1,0:T(8,128)(2,1)S(1)}, bf16[960,128]{1,0:T(8,128)(2,1)S(1)}, u32[]{:S(2)}, u32[]{:S(2)}) %collective-permute-start.1) | collective-permute-done | bytes 245792 | tf_op jit(solution)/shard_map/ppermute | solution.py:81
  271.3 0.7 copy.44
  (30 shorter events, 0.6 us)
Async XLA Ops:
  6.5 1.8 copy-start
  6.5 98.5 %all-gather.2.cloned.1.call-start = ((), (), s32[]{:S(2)}) async-start(), calls=%async_computation.4 | async-start | bytes 8847360 | tf_op jit(solution)/shard_map/all_gather | solution.py:47
  32.6 72.5 %all-to-all-start = ((bf16[120,32,480]{2,0,1:T(8,128)(2,1)}), bf16[120,32,480]{2,0,1:T(8,128)(2,1)}, u32[]{:S(2)}, u32[]{:S(2)}) async-start(bf16[120,32,480]{2,0,1:T(8,128)(2,1)} %copy.32), calls=%async_computation | async-start | bytes 7864320 | tf_op jit(solution)/shard_map/all_to_all | solution.py:58
  120.9 54.7 %all-to-all-start.1 = ((bf16[120,32,480]{0,2,1:T(8,128)(2,1)}), bf16[120,32,480]{0,2,1:T(8,128)(2,1)}, u32[]{:S(2)}, u32[]{:S(2)}) async-start(bf16[120,32,480]{0,2,1:T(8,128)(2,1)} %bitcast.22), calls=%async_computation.2 | async-start | bytes 7864320 | tf_op jit(solution)/shard_map/all_to_all | solution.py:58
  128.0 98.7 %reduce-scatter.3.cloned.1.call-start = ((), (), s32[]{:S(2)}) async-start(), calls=%async_computation.5 | async-start | bytes 2211840 | tf_op jit(solution)/shard_map/reduce_scatter | solution.py:57
  128.7 117.3 %reduce-scatter.5.cloned.1.call-start = ((), (), s32[]{:S(2)}) async-start(), calls=%async_computation.6 | async-start | bytes 2211840 | tf_op jit(solution)/shard_map/reduce_scatter | solution.py:62
  189.8 9.8 %copy-start.5 = (bf16[960,128]{1,0:T(8,128)(2,1)S(1)}, bf16[960,128]{1,0:T(8,128)(2,1)}, u32[]{:S(2)}) copy-start(bf16[960,128]{1,0:T(8,128)(2,1)} %param.11) | copy-start | bytes 737284
  189.8 16.4 %copy-start.1 = (f32[192]{0:T(256)S(1)}, f32[192]{0:T(256)}, u32[]{:S(2)}) copy-start(f32[192]{0:T(256)} %param.15) | copy-start | bytes 2308
  189.8 16.5 %copy-start.2 = (f32[240]{0:T(256)S(1)}, f32[240]{0:T(256)}, u32[]{:S(2)}) copy-start(f32[240]{0:T(256)} %param.14) | copy-start | bytes 2884
  189.8 17.2 %copy-start.3 = (s32[192]{0:T(256)S(1)}, s32[192]{0:T(256)}, u32[]{:S(2)}) copy-start(s32[192]{0:T(256)} %param.13) | copy-start | bytes 2308
  189.8 17.3 %copy-start.4 = (s32[240]{0:T(256)S(1)}, s32[240]{0:T(256)}, u32[]{:S(2)}) copy-start(s32[240]{0:T(256)} %param.12) | copy-start | bytes 2884
  199.6 27.1 %collective-permute-start = (bf16[960,128]{1,0:T(8,128)(2,1)S(1)}, bf16[960,128]{1,0:T(8,128)(2,1)S(1)}, u32[]{:S(2)}, u32[]{:S(2)}) collective-permute-start(bf16[960,128]{1,0:T(8,128)(2,1)S(1)} %copy-done.5), channel_id=1, source_target_pairs={{0,0},{1,32},{2,64},{3,96},{4,128},{5,160},{6,192},{7,224},{32,1},... | collective-permute-start | bytes 737288 | tf_op jit(solution)/shard_map/ppermute | solution.py:65
  247.4 23.9 %collective-permute-start.1 = (bf16[960,128]{1,0:T(8,128)(2,1)S(1)}, bf16[960,128]{1,0:T(8,128)(2,1)S(1)}, u32[]{:S(2)}, u32[]{:S(2)}) collective-permute-start(bf16[960,128]{1,0:T(8,128)(2,1)S(1)} %fusion.2), channel_id=1, source_target_pairs={{0,0},{1,32},{2,64},{3,96},{4,128},{5,160},{6,192},{7,224},{32,1},... | collective-permute-start | bytes 737288 | tf_op jit(solution)/shard_map/ppermute | solution.py:81
Sparse Core Ops, SparseCore 0:
  10.5 87.8 all-gather.1
  131.4 38.8 reduce-scatter.2
  199.7 46.2 reduce-scatter.4
where the time goes:
time: 280 us; the launch traced here: 278 us
  waiting for transfers between devices  161 us (58%)
  local copies, waits for them, and re-layouts  53.2 us (19%)
  starting transfers between devices  28.7 us (10%)
  matrix products  19.4 us (7%)
  between operations  13.3 us (5%)
  other arithmetic  3.02 us (1%)
    all_to_all x2, waiting for transfers between devices, local(): lax.all_to_all(piece, (X, C, Y), split_axis=1, concat_axis=0, tiled=True)  105 us
    all_to_all x4, local copies, waits for them, and re-layouts, local(): lax.all_to_all(piece, (X, C, Y), split_axis=1, concat_axis=0, tiled=True)  26.8 us
    dot_general x2, matrix products, local(): lax.dot_general(plane_amps, masked_all, (((0,), (0,)), ((), ())), preferr...  19.4 us
    reduce_scatter x2, waiting for transfers between devices, local(): sums.append(lax.psum_scatter(previous, Z, scatter_dimension=1, tiled=True))  19.3 us
    ppermute x1, waiting for transfers between devices, local(): coulomb_here = lax.ppermute(coulomb, (Z, X, C), perm)  18.8 us
    ppermute x1, waiting for transfers between devices, local(): return lax.ppermute(out, (Z, X, C), perm)  16.7 us
    all_to_all x2, starting transfers between devices, local(): lax.all_to_all(piece, (X, C, Y), split_axis=1, concat_axis=0, tiled=True)  14.8 us
    unnamed x15, local copies, waits for them, and re-layouts  11.4 us
  transfers between devices with their start and end apart: 7, of which 5 were waited for; matrix products, arithmetic and copies ran while one was open for 16% of the time, Pallas kernels for 0%

commit v1 on v0

--- a/solution.py
+++ b/solution.py
@@ -55,7 +55,12 @@
         if previous is not None:
             previous, piece = lax.optimization_barrier((previous, piece))
             sums.append(lax.psum_scatter(previous, Z, scatter_dimension=1, tiled=True))
-        plane_amps = lax.all_to_all(piece, (X, C, Y), split_axis=1, concat_axis=0, tiled=True)
+        plane_amps = jnp.concatenate(
+            lax.all_to_all(
+                jnp.stack(jnp.split(piece, lax.axis_size((X, C, Y)), axis=1)), (X, C, Y), 0, 0
+            ),
+            axis=0,
+        )
         previous = lax.dot_general(
             plane_amps, masked_all, (((0,), (0,)), ((), ())), preferred_element_type=jnp.float32
         )

time: 280 us -> 369 us (1.32)
  local copies, waits for them, and re-layouts: 53.2 us -> 159 us
  waiting for transfers between devices: 161 us -> 143 us
    unnamed x15 -> x80, local copies, waits for them, and re-layouts: 11.4 us -> 75.9 us
    slice x1, local copies, waits for them, and re-layouts: 5.67 us -> 38.6 us  [local(): piece = pieces[:, :, k, :].reshape(sub, groups * width)]
    all_to_all x4 -> x0, local copies, waits for them, and re-layouts: 26.8 us -> none  [local(): lax.all_to_all(piece, (X, C, Y), split_axis=1, concat_axis=0, tiled=True)]
    reshape x0 -> x1, local copies, waits for them, and re-layouts: none -> 22.8 us  [local(): pieces = amps.reshape(sub, groups, CHUNKS, width)]
    all_to_all x2, waiting for transfers between devices: 105 us -> 85.9 us  [local(): lax.all_to_all(jnp.stack(jnp.split(piece, lax.axis_size((X, C, Y)), axis=...]
    another operation x1 -> x2, local copies, waits for them, and re-layouts: 6.2 us -> 17 us  [local(): piece = pieces[:, :, k, :].reshape(sub, groups * width)]
  transfers between devices with their start and end apart: 7 -> 7, of which waited for: 5 -> 5; matrix products, arithmetic and copies ran while one was open for 16% -> 35% of each run, Pallas kernels for 0% -> 0%
where the time goes in v1:
time: 369 us; the launch traced here: 368 us
  local copies, waits for them, and re-layouts  159 us (43%)
  waiting for transfers between devices  143 us (39%)
  starting transfers between devices  29.9 us (8%)
  matrix products  19.5 us (5%)
  between operations  13.3 us (4%)
    all_to_all x2, waiting for transfers between devices, local(): lax.all_to_all(jnp.stack(jnp.split(piece, lax.axis_size((X, C, Y)), axis=...  85.9 us
    unnamed x80, local copies, waits for them, and re-layouts  75.9 us
    slice x1, local copies, waits for them, and re-layouts, local(): piece = pieces[:, :, k, :].reshape(sub, groups * width)  38.6 us
    reshape x1, local copies, waits for them, and re-layouts, local(): pieces = amps.reshape(sub, groups, CHUNKS, width)  22.8 us
    dot_general x2, matrix products, local(): lax.dot_general(plane_amps, masked_all, (((0,), (0,)), ((), ())), preferr...  19.5 us
    ppermute x1, waiting for transfers between devices, local(): coulomb_here = lax.ppermute(coulomb, (Z, X, C), perm)  19.1 us
    reduce_scatter x2, waiting for transfers between devices, local(): sums.append(lax.psum_scatter(previous, Z, scatter_dimension=1, tiled=True))  19 us
    ppermute x1, waiting for transfers between devices, local(): return lax.ppermute(out, (Z, X, C), perm)  18.1 us
  transfers between devices with their start and end apart: 7, of which 5 were waited for; matrix products, arithmetic and copies ran while one was open for 35% of the time, Pallas kernels for 0%

profile of v1, /device:TPU:31, one launch (start us, length us, event | category | flops | bytes accessed | tf_op | source)
XLA Modules:
  0.0 367.5 jit_solution(6746122183675165202)
XLA Ops:
  10.4 22.8 %reshape.125 = bf16[120,32,2,480]{3,2,1,0:T(2,128)(2,1)} reshape(bf16[120,30720]{1,0:T(8,128)(2,1)} %param.8) | data formatting | bytes 14745600 | tf_op jit(solution)/shard_map/reshape | solution.py:50
  33.2 38.6 %slice_reduce_fusion = (bf16[120,32,480]{2,1,0:T(8,128)(2,1)}, bf16[120,32,480]{2,1,0:T(8,128)(2,1)}) fusion(bf16[120,32,2,480]{3,2,1,0:T(2,128)(2,1)} %reshape.125), kind=kLoop, calls=%fused_computation | loop fusion | bytes 14745600 | tf_op jit(solution)/shard_map/slice | solution.py:54
  71.8 8.5 %reshape_squeeze.6 = bf16[120,15360]{1,0:T(8,128)(2,1)} reshape(bf16[120,32,480]{2,1,0:T(8,128)(2,1)} %get-tuple-element.10) | data formatting | bytes 7372800 | tf_op jit(solution)/shard_map/reshape;squeeze | solution.py:54
  80.3 1.7 constant_dynamic-update-slice_fusion.31
  82.0 1.7 constant_dynamic-update-slice_fusion.30
  85.3 1.7 constant_dynamic-update-slice_fusion.28
  88.5 1.7 constant_dynamic-update-slice_fusion.26
  91.9 1.7 constant_dynamic-update-slice_fusion.24
  96.8 1.7 constant_dynamic-update-slice_fusion.21
  101.7 1.7 constant_dynamic-update-slice_fusion.18
  103.3 1.7 constant_dynamic-update-slice_fusion.17
  105.0 1.7 constant_dynamic-update-slice_fusion.16
  118.3 7.7 %all-to-all-start = ((bf16[32,120,480]{2,1,0:T(8,128)(2,1)}), bf16[32,120,480]{2,1,0:T(8,128)(2,1)}, u32[]{:S(2)}, u32[]{:S(2)}) async-start(bf16[32,120,480]{2,1,0:T(8,128)(2,1)} %constant_dynamic-update-slice_fusion), calls=%async_computation | async-start | bytes 7864320 | tf_op jit(solution)/shard_map/all_to_all | solution.py:59
  126.0 8.5 %reshape_squeeze.7 = bf16[120,15360]{1,0:T(8,128)(2,1)} reshape(bf16[120,32,480]{2,1,0:T(8,128)(2,1)} %get-tuple-element.9) | data formatting | bytes 7372800 | tf_op jit(solution)/shard_map/reshape;squeeze | solution.py:54
  134.5 39.1 %all-to-all-done = bf16[32,120,480]{2,1,0:T(8,128)(2,1)} async-done(((bf16[32,120,480]{2,1,0:T(8,128)(2,1)}), bf16[32,120,480]{2,1,0:T(8,128)(2,1)}, u32[]{:S(2)}, u32[]{:S(2)}) %all-to-all-start) | async-done | bytes 3686432 | tf_op jit(solution)/shard_map/all_to_all | solution.py:59
  173.6 9.7 %fusion.12 = f32[480,1024]{1,0:T(8,128)} fusion(bf16[3840,480]{1,0:T(8,128)(2,1)} %bitcast.32, bf16[3840,1024]{1,0:T(8,128)(2,1)} %all-gather.2.cloned.1.call-done), kind=kOutput, calls=%fused_computation.143 | convolution fusion | flops 3774873600 | bytes 13516800 | tf_op jit(solution)/shard_map/dot_general | solution.py:64
  183.3 1.7 constant_dynamic-update-slice_fusion.63
  185.0 1.7 constant_dynamic-update-slice_fusion.62
  191.6 1.7 constant_dynamic-update-slice_fusion.58
  194.9 1.7 constant_dynamic-update-slice_fusion.56
  199.8 1.7 constant_dynamic-update-slice_fusion.53
  204.7 1.7 constant_dynamic-update-slice_fusion.50
  206.4 1.7 constant_dynamic-update-slice_fusion.49
  208.1 1.7 constant_dynamic-update-slice_fusion.48
  221.4 7.4 %all-to-all-start.1 = ((bf16[32,120,480]{2,1,0:T(8,128)(2,1)}), bf16[32,120,480]{2,1,0:T(8,128)(2,1)}, u32[]{:S(2)}, u32[]{:S(2)}) async-start(bf16[32,120,480]{2,1,0:T(8,128)(2,1)} %constant_dynamic-update-slice_fusion.32), calls=%async_computation.2 | async-start | bytes 7864320 | tf_op jit(solution)/shard_map/all_to_all | solution.py:59
  229.6 46.8 %all-to-all-done.1 = bf16[32,120,480]{2,1,0:T(8,128)(2,1)} async-done(((bf16[32,120,480]{2,1,0:T(8,128)(2,1)}), bf16[32,120,480]{2,1,0:T(8,128)(2,1)}, u32[]{:S(2)}, u32[]{:S(2)}) %all-to-all-start.1) | async-done | bytes 3686432 | tf_op jit(solution)/shard_map/all_to_all | solution.py:59
  276.5 9.8 %fusion.13 = f32[480,1024]{1,0:T(8,128)} fusion(bf16[3840,480]{1,0:T(8,128)(2,1)} %bitcast.66, bf16[3840,1024]{1,0:T(8,128)(2,1)} %all-gather.2.cloned.1.call-done), kind=kOutput, calls=%fused_computation.144 | convolution fusion | flops 3774873600 | bytes 13516800 | tf_op jit(solution)/shard_map/dot_general | solution.py:64
  286.3 9.0 %collective-permute-start = (bf16[960,128]{1,0:T(8,128)(2,1)S(1)}, bf16[960,128]{1,0:T(8,128)(2,1)S(1)}, u32[]{:S(2)}, u32[]{:S(2)}) collective-permute-start(bf16[960,128]{1,0:T(8,128)(2,1)S(1)} %copy-done.7), channel_id=1, source_target_pairs={{0,0},{1,32},{2,64},{3,96},{4,128},{5,160},{6,192},{7,224},{32,1},... | collective-permute-start | bytes 737288 | tf_op jit(solution)/shard_map/ppermute | solution.py:70
  296.9 19.1 %collective-permute-done = bf16[960,128]{1,0:T(8,128)(2,1)S(1)} collective-permute-done((bf16[960,128]{1,0:T(8,128)(2,1)S(1)}, bf16[960,128]{1,0:T(8,128)(2,1)S(1)}, u32[]{:S(2)}, u32[]{:S(2)}) %collective-permute-start) | collective-permute-done | bytes 245792 | tf_op jit(solution)/shard_map/ppermute | solution.py:70
  316.0 19.0 %reduce-scatter.5.cloned.1.call-done = f32[480,128]{1,0:T(8,128)} async-done(((f32[480,1024]{1,0:T(8,128)}), f32[480,128]{1,0:T(8,128)}) %reduce-scatter.5.cloned.1.call-update) | async-done | bytes 245776 | tf_op jit(solution)/shard_map/reduce_scatter | solution.py:67
  336.4 5.8 %collective-permute-start.1 = (bf16[960,128]{1,0:T(8,128)(2,1)S(1)}, bf16[960,128]{1,0:T(8,128)(2,1)S(1)}, u32[]{:S(2)}, u32[]{:S(2)}) collective-permute-start(bf16[960,128]{1,0:T(8,128)(2,1)S(1)} %fusion.2), channel_id=1, source_target_pairs={{0,0},{1,32},{2,64},{3,96},{4,128},{5,160},{6,192},{7,224},{32,1},... | collective-permute-start | bytes 737288 | tf_op jit(solution)/shard_map/ppermute | solution.py:86
  342.2 18.1 %collective-permute-done.1 = bf16[960,128]{1,0:T(8,128)(2,1)S(1)} collective-permute-done((bf16[960,128]{1,0:T(8,128)(2,1)S(1)}, bf16[960,128]{1,0:T(8,128)(2,1)S(1)}, u32[]{:S(2)}, u32[]{:S(2)}) %collective-permute-start.1) | collective-permute-done | bytes 245792 | tf_op jit(solution)/shard_map/ppermute | solution.py:86
  (95 shorter events, 55.9 us)
Async XLA Ops:
  6.5 1.8 copy-start.2
  6.5 167.1 %all-gather.2.cloned.1.call-start = ((), (), s32[]{:S(2)}) async-start(), calls=%async_computation.4 | async-start | bytes 8847360 | tf_op jit(solution)/shard_map/all_gather | solution.py:47
  80.3 26.4 %copy-start.1 = (bf16[120,15360]{1,0:T(8,128)(2,1)S(1)}, bf16[120,15360]{1,0:T(8,128)(2,1)}, u32[]{:S(2)}) copy-start(bf16[120,15360]{1,0:T(8,128)(2,1)} %reshape_squeeze.6) | copy-start | bytes 11059204
  118.3 55.3 %all-to-all-start = ((bf16[32,120,480]{2,1,0:T(8,128)(2,1)}), bf16[32,120,480]{2,1,0:T(8,128)(2,1)}, u32[]{:S(2)}, u32[]{:S(2)}) async-start(bf16[32,120,480]{2,1,0:T(8,128)(2,1)} %constant_dynamic-update-slice_fusion), calls=%async_computation | async-start | bytes 7864320 | tf_op jit(solution)/shard_map/all_to_all | solution.py:59
  183.3 26.4 %copy-start = (bf16[120,15360]{1,0:T(8,128)(2,1)S(1)}, bf16[120,15360]{1,0:T(8,128)(2,1)}, u32[]{:S(2)}) copy-start(bf16[120,15360]{1,0:T(8,128)(2,1)} %reshape_squeeze.7) | copy-start | bytes 11059204
  221.4 55.0 %all-to-all-start.1 = ((bf16[32,120,480]{2,1,0:T(8,128)(2,1)}), bf16[32,120,480]{2,1,0:T(8,128)(2,1)}, u32[]{:S(2)}, u32[]{:S(2)}) async-start(bf16[32,120,480]{2,1,0:T(8,128)(2,1)} %constant_dynamic-update-slice_fusion.32), calls=%async_computation.2 | async-start | bytes 7864320 | tf_op jit(solution)/shard_map/all_to_all | solution.py:59
  228.8 87.2 %reduce-scatter.3.cloned.1.call-start = ((), (), s32[]{:S(2)}) async-start(), calls=%async_computation.5 | async-start | bytes 2211840 | tf_op jit(solution)/shard_map/reduce_scatter | solution.py:57
  229.6 105.5 %reduce-scatter.5.cloned.1.call-start = ((), (), s32[]{:S(2)}) async-start(), calls=%async_computation.6 | async-start | bytes 2211840 | tf_op jit(solution)/shard_map/reduce_scatter | solution.py:67
  276.4 9.9 %copy-start.7 = (bf16[960,128]{1,0:T(8,128)(2,1)S(1)}, bf16[960,128]{1,0:T(8,128)(2,1)}, u32[]{:S(2)}) copy-start(bf16[960,128]{1,0:T(8,128)(2,1)} %param.11) | copy-start | bytes 737284
  276.4 18.9 %copy-start.3 = (f32[240]{0:T(256)S(1)}, f32[240]{0:T(256)}, u32[]{:S(2)}) copy-start(f32[240]{0:T(256)} %param.14) | copy-start | bytes 2884
  276.4 19.0 %copy-start.4 = (f32[192]{0:T(256)S(1)}, f32[192]{0:T(256)}, u32[]{:S(2)}) copy-start(f32[192]{0:T(256)} %param.15) | copy-start | bytes 2308
  276.4 19.2 %copy-start.5 = (s32[192]{0:T(256)S(1)}, s32[192]{0:T(256)}, u32[]{:S(2)}) copy-start(s32[192]{0:T(256)} %param.13) | copy-start | bytes 2308
  276.4 19.8 %copy-start.6 = (s32[240]{0:T(256)S(1)}, s32[240]{0:T(256)}, u32[]{:S(2)}) copy-start(s32[240]{0:T(256)} %param.12) | copy-start | bytes 2884
  286.3 29.7 %collective-permute-start = (bf16[960,128]{1,0:T(8,128)(2,1)S(1)}, bf16[960,128]{1,0:T(8,128)(2,1)S(1)}, u32[]{:S(2)}, u32[]{:S(2)}) collective-permute-start(bf16[960,128]{1,0:T(8,128)(2,1)S(1)} %copy-done.7), channel_id=1, source_target_pairs={{0,0},{1,32},{2,64},{3,96},{4,128},{5,160},{6,192},{7,224},{32,1},... | collective-permute-start | bytes 737288 | tf_op jit(solution)/shard_map/ppermute | solution.py:70
  336.4 23.9 %collective-permute-start.1 = (bf16[960,128]{1,0:T(8,128)(2,1)S(1)}, bf16[960,128]{1,0:T(8,128)(2,1)S(1)}, u32[]{:S(2)}, u32[]{:S(2)}) collective-permute-start(bf16[960,128]{1,0:T(8,128)(2,1)S(1)} %fusion.2), channel_id=1, source_target_pairs={{0,0},{1,32},{2,64},{3,96},{4,128},{5,160},{6,192},{7,224},{32,1},... | collective-permute-start | bytes 737288 | tf_op jit(solution)/shard_map/ppermute | solution.py:86
Sparse Core Ops, SparseCore 0:
  10.5 51.3 all-gather.1
  232.2 39.9 reduce-scatter.2
  286.4 48.5 reduce-scatter.4
